TPU v7x, 32 devices: a whole 2x2x4 slice. The times are simulated.
32 devices in a mesh: space: 8 (over z, x), fsdp: 4 (over y, core).
Axes of the slice: x: 2, y: 2, z: 4, core: 2. Of those that a mesh axis runs over, the one named last changes fastest.
Arguments:
- features: bfloat16 [4, 128, 8, 8, 512], P('fsdp', 'space'), may hold values from -6 to 6
- cotangent: bfloat16 [4, 128, 8, 8, 512], P('fsdp', 'space'), may hold values from -6 to 6
- tissue: int32 [4, 128], P('fsdp', 'space'), may hold values 0 or 1
- weight: bfloat16 [27, 64, 64], P(None, 'fsdp'), may hold values from -0.15625 to 0.15625
Outputs:
- activations: bfloat16 [4, 128, 8, 8, 512], P('fsdp', 'space')
- input_grad: bfloat16 [4, 128, 8, 8, 512], P('fsdp', 'space')
- weight_grad: float32 [27, 64, 64], P(None, 'fsdp')
All inputs are finite; a program needn't handle non-finite values. No bound on the sum of `tissue` on one device may be relied on, other than what follows from the above.
Results may differ from a plain program's by a relative error of at most 0.0034.
Values may be sent and summed in bfloat16 or wider, within the bound.
No kernel may reach another device: no remote copies, remote signals or barrier semaphores. Data moves between devices by JAX's collectives and lax.ppermute only.
A program may use at most 192 MiB of HBM per device.

v0:
```python
import math

import jax
import jax.numpy as jnp
from jax import lax
from jax.sharding import PartitionSpec as P

BRICK_X = 2
BRICK_Y = 2
BRICK_Z = 4


def from_behind(shard, axis, by):
    peers = lax.axis_size(axis)
    pairs = [(i, i + by) for i in range(peers) if 0 <= i + by < peers]
    return lax.ppermute(shard, axis, pairs)


def grid_shape(number):
    factors = [1, 1, 1]
    places = 0
    while number % 2 == 0:
        factors[places % 3] = factors[places % 3] * 2
        number = number // 2
        places = places + 1
    factors[0] = factors[0] * number
    return factors


def to_volume(bricks, edge_cells, channels):
    blocks = bricks.reshape(
        BRICK_X, BRICK_Y, BRICK_Z, edge_cells, edge_cells, edge_cells * channels
    )
    blocks = blocks.transpose(0, 3, 1, 4, 2, 5)
    return blocks.reshape(
        BRICK_X * edge_cells, BRICK_Y * edge_cells, BRICK_Z * edge_cells * channels
    )


def to_bricks(volume, edge_cells, channels):
    blocks = volume.reshape(
        BRICK_X, edge_cells, BRICK_Y, edge_cells, BRICK_Z, edge_cells * channels
    )
    blocks = blocks.transpose(0, 2, 4, 1, 3, 5)
    return blocks.reshape(
        BRICK_X * BRICK_Y * BRICK_Z, edge_cells, edge_cells, edge_cells * channels
    )


def neighbour_plane(portion, offset, present):
    arrived = from_behind(portion, "space", offset)
    return jnp.where(present, arrived, jnp.zeros_like(arrived))


def extend_segmented(volume, grid_dims, places, channels):
    strides = (grid_dims[1] * grid_dims[2], grid_dims[2], 1)
    unit_sizes = (1, 1, channels)
    for axis_pos in range(3):
        extent = volume.shape[axis_pos]
        width_now = unit_sizes[axis_pos]
        last_layer = lax.slice_in_dim(volume, extent - width_now, extent, axis=axis_pos)
        first_layer = lax.slice_in_dim(volume, 0, width_now, axis=axis_pos)
        from_below = neighbour_plane(last_layer, strides[axis_pos], places[axis_pos] > 0)
        from_above = neighbour_plane(
            first_layer, -strides[axis_pos], places[axis_pos] < grid_dims[axis_pos] - 1
        )
        volume = jnp.concatenate([from_below, volume, from_above], axis=axis_pos)
    return volume


def tap_rows(padded, tap_index, shape_out):
    size_x, size_y, size_z = shape_out
    shift_x = tap_index // 9
    shift_y = tap_index // 3 % 3
    shift_z = tap_index % 3
    window = padded[
        shift_x : shift_x + size_x, shift_y : shift_y + size_y, shift_z : shift_z + size_z, :
    ]
    return window.reshape(size_x * size_y * size_z, padded.shape[-1])


def correlate(padded, taps, shape_out):
    size_x, size_y, size_z = shape_out
    total = jnp.zeros((size_x * size_y * size_z, taps.shape[2]), jnp.float32)
    for tap_index in range(27):
        total = total + jnp.dot(
            tap_rows(padded, tap_index, shape_out),
            taps[tap_index],
            preferred_element_type=jnp.float32,
        )
    return total.reshape(size_x, size_y, size_z * taps.shape[2])


def weight_terms(padded, grad_volume, shape_out):
    size_x, size_y, size_z = shape_out
    channels = padded.shape[-1]
    grad_rows = grad_volume.reshape(size_x * size_y * size_z, channels)
    pieces = []
    for tap_index in range(27):
        rows_in = tap_rows(padded, tap_index, shape_out)
        pieces.append(
            lax.dot_general(
                rows_in, grad_rows, (((0,), (0,)), ((), ())), preferred_element_type=jnp.float32
            )
        )
    return jnp.stack(pieces)


def local(features, cotangent, tissue, weight):
    edge_cells = features.shape[2]
    channels = weight.shape[2]
    grid_dims = grid_shape(lax.axis_size("space"))
    index_now = lax.axis_index("space")
    places = (
        index_now // (grid_dims[1] * grid_dims[2]),
        index_now // grid_dims[2] % grid_dims[1],
        index_now % grid_dims[2],
    )
    size_x = BRICK_X * edge_cells
    size_y = BRICK_Y * edge_cells
    size_z = BRICK_Z * edge_cells
    shape_out = (size_x, size_y, size_z)
    weight_full = lax.all_gather(weight, "fsdp", axis=1, tiled=True)
    kernel_back = jnp.flip(weight_full, 0).transpose(0, 2, 1)
    tissue_mask = tissue[0].astype(jnp.float32)[:, None, None, None]
    inputs = features[0]
    incoming = cotangent[0].astype(jnp.float32)
    masked = jnp.where(tissue[0][:, None, None, None] > 0, inputs, jnp.zeros_like(inputs))

    def padded_of(bricks):
        volume = to_volume(bricks, edge_cells, channels)
        grown = extend_segmented(volume, grid_dims, places, channels)
        return grown.reshape(size_x + 2, size_y + 2, size_z + 2, channels)

    padded_in = padded_of(masked)
    pre_act = to_bricks(correlate(padded_in, weight_full, shape_out), edge_cells, channels)
    gate_val = jax.nn.sigmoid(pre_act)
    activations = (tissue_mask * (inputs.astype(jnp.float32) + pre_act * gate_val)).astype(
        jnp.bfloat16
    )
    slope = gate_val * (1.0 + pre_act * (1.0 - gate_val))
    grad_pre = (tissue_mask * incoming * slope).astype(jnp.bfloat16)
    padded_grad = padded_of(grad_pre)
    back_conv = to_bricks(correlate(padded_grad, kernel_back, shape_out), edge_cells, channels)
    input_grad = (tissue_mask * (incoming + back_conv)).astype(jnp.bfloat16)
    grad_volume = to_volume(grad_pre, edge_cells, channels)
    total_cells = (
        lax.axis_size("space") * lax.axis_size("fsdp") * BRICK_X * BRICK_Y * BRICK_Z * edge_cells**3
    )
    grad_term = weight_terms(padded_in, grad_volume, shape_out) / math.sqrt(total_cells)
    grad_whole = lax.psum(grad_term, ("space", "fsdp"))
    rows_each = channels // lax.axis_size("fsdp")
    grad_part = lax.dynamic_slice_in_dim(
        grad_whole, lax.axis_index("fsdp") * rows_each, rows_each, 1
    )
    return (activations[None], input_grad[None], grad_part)


def solution(mesh):
    return jax.shard_map(
        local,
        mesh=mesh,
        in_specs=(
            P("fsdp", "space", None, None, None),
            P("fsdp", "space", None, None, None),
            P("fsdp", "space"),
            P(None, "fsdp", None),
        ),
        out_specs=(
            P("fsdp", "space", None, None, None),
            P("fsdp", "space", None, None, None),
            P(None, "fsdp", None),
        ),
        check_vma=False,
    )
```

profile of v0, /device:TPU:0, one launch (start us, length us, event | category | flops | bytes accessed | tf_op | source)
XLA Modules:
  0.0 354.7 jit_solution(6567755432332149316)
XLA Ops:
  8.0 2.1 fusion.34
  10.9 6.0 %collective-permute-start = (bf16[1,16,2048]{2,1,0:T(8,128)(2,1)S(1)}, bf16[1,16,2048]{2,1,0:T(8,128)(2,1)S(1)}, u32[]{:S(2)}, u32[]{:S(2)}) collective-permute-start(bf16[1,16,2048]{2,1,0:T(8,128)(2,1)S(1)} %get-tuple-element.67), channel_id=1, source_target_pairs={{0,16},{4,20},{8,24},{12,28},{1,17},{5,21},{9,25},{13,29},{2,18},{... | collective-permute-start | bytes 196616 | tf_op jit(solution)/shard_map/ppermute | solution.py:16
  18.8 6.7 %all_gather.3 = bf16[27,64,64]{2,1,0:T(8,128)(2,1)S(1)} all-gather(bf16[27,16,64]{2,1,0:T(8,128)(2,1)S(1)} %copy-done.83), channel_id=1, replica_groups=mesh['space'=8,'fsdp'=4] {'fsdp'}, dimensions={1}, use_global_device_ids=true | all-gather | bytes 276480 | tf_op jit(solution)/shard_map/all_gather | solution.py:123
  25.8 3.5 collective-permute-start.2
  33.1 5.5 %collective-permute-done.3 = bf16[18,1,2048]{2,1,0:T(2,128)(2,1)S(1)} collective-permute-done((bf16[18,1,2048]{2,1,0:T(2,128)(2,1)S(1)}, bf16[18,1,2048]{2,1,0:T(2,128)(2,1)S(1)}, u32[]{:S(2)}, u32[]{:S(2)}) %collective-permute-start.3) | collective-permute-done | bytes 73760 | tf_op jit(solution)/shard_map/ppermute | solution.py:16
  41.3 4.5 %collective-permute-start.4 = (bf16[18,18,64]{2,1,0:T(8,128)(2,1)S(1)}, bf16[18,18,64]{2,1,0:T(8,128)(2,1)S(1)}, u32[]{:S(2)}, u32[]{:S(2)}) collective-permute-start(bf16[18,18,64]{2,1,0:T(8,128)(2,1)S(1)} %get-tuple-element.60), channel_id=1, source_target_pairs={{0,4},{4,8},{8,12},{12,16},{16,20},{20,24},{24,28},{1,5},{5,9},{9,... | collective-permute-start | bytes 124424 | tf_op jit(solution)/shard_map/ppermute | solution.py:16
  46.5 2.2 collective-permute-done.4
  48.7 3.2 concatenate.20
  51.8 4.4 %reshape.271 = bf16[18,18,34,64]{3,2,1,0:T(8,128)(2,1)S(1)} reshape(bf16[18,18,2176]{2,1,0:T(8,128)(2,1)} %concatenate.20) | data formatting | bytes 2820096 | tf_op jit(solution)/shard_map/reshape | solution.py:133
  56.2 13.2 %fusion.40 = (bf16[16,16,32,64]{3,2,1,0:T(8,128)(2,1)S(1)}, bf16[16,16,32,64]{3,2,1,0:T(8,128)(2,1)S(1)}, bf16[16,16,32,64]{3,2,1,0:T(8,128)(2,1)S(1)}, bf16[16,...) fusion(bf16[18,18,34,64]{3,2,1,0:T(8,128)(2,1)S(1)} %reshape.271), kind=kLoop, calls=%fused_computation.204 | loop fusion | bytes 39845888 | tf_op jit(solution)/shard_map/slice | solution.py:76
  69.5 7.7 %fusion.41 = (bf16[16,16,32,64]{3,2,1,0:T(8,128)(2,1)S(1)}, bf16[16,16,32,64]{3,2,1,0:T(8,128)(2,1)S(1)}, bf16[16,16,32,64]{3,2,1,0:T(8,128)(2,1)}, bf16[16,16,3...) fusion(bf16[18,18,34,64]{3,2,1,0:T(8,128)(2,1)S(1)} %reshape.271), kind=kLoop, calls=%fused_computation.205 | loop fusion | bytes 16777216 | tf_op jit(solution)/shard_map/slice | solution.py:76
  77.2 4.0 %fusion.37 = f32[8192,64]{0,1:T(8,128)S(1)} fusion(bf16[8192,64]{1,0:T(8,128)(2,1)} %bitcast.520, bf16[27,64,64]{2,1,0:T(8,128)(2,1)S(1)} %copy-done.81), kind=kOutput, calls=%fused_computation.197 | convolution fusion | flops 67108864 | bytes 3162112 | tf_op jit(solution)/shard_map/dot_general | solution.py:86
  115.1 13.0 %convolution_add_fusion.28 = f32[8192,64]{0,1:T(8,128)S(1)} fusion(f32[8192,64]{0,1:T(8,128)S(1)} %convolution_add_fusion.29, bf16[8192,64]{1,0:T(8,128)(2,1)S(1)} %bitcast.472, bf16[27,64,64]{2,1,0:T(8,128)(2,1)S(1)} %copy-done.81), kind=kOutput, calls=%fused_computation.28 | convolution fusion | flops 67633152 | bytes 6307840 | tf_op jit(solution)/shard_map/dot_general | solution.py:86
  129.9 2.8 copy.17
  132.7 3.8 %reshape_reshape.9 = f32[2,8,2,8,4,512]{5,4,3,2,1,0:T(4,128)S(1)} reshape(f32[8192,64]{1,0:T(8,128)} %copy.17) | data formatting | bytes 4194304 | tf_op jit(solution)/shard_map/reshape;reshape | solution.py:41
  139.5 3.0 reshape_reshape.11
  144.3 2.4 fusion.33
  184.2 6.9 %collective-permute-start.6 = (bf16[1,16,2048]{2,1,0:T(8,128)(2,1)S(1)}, bf16[1,16,2048]{2,1,0:T(8,128)(2,1)S(1)}, u32[]{:S(2)}, u32[]{:S(2)}) collective-permute-start(bf16[1,16,2048]{2,1,0:T(8,128)(2,1)S(1)} %get-tuple-element.65), channel_id=1, source_target_pairs={{0,16},{4,20},{8,24},{12,28},{1,17},{5,21},{9,25},{13,29},{2,18},{... | collective-permute-start | bytes 196616 | tf_op jit(solution)/shard_map/ppermute | solution.py:16
  193.2 5.7 %collective-permute-done.7 = bf16[1,16,2048]{2,1,0:T(8,128)(2,1)S(1)} collective-permute-done((bf16[1,16,2048]{2,1,0:T(8,128)(2,1)S(1)}, bf16[1,16,2048]{2,1,0:T(8,128)(2,1)S(1)}, u32[]{:S(2)}, u32[]{:S(2)}) %collective-permute-start.7) | collective-permute-done | bytes 65568 | tf_op jit(solution)/shard_map/ppermute | solution.py:16
  199.1 3.5 collective-permute-start.8
  205.4 4.9 %collective-permute-done.9 = bf16[18,1,2048]{2,1,0:T(2,128)(2,1)S(1)} collective-permute-done((bf16[18,1,2048]{2,1,0:T(2,128)(2,1)S(1)}, bf16[18,1,2048]{2,1,0:T(2,128)(2,1)S(1)}, u32[]{:S(2)}, u32[]{:S(2)}) %collective-permute-start.9) | collective-permute-done | bytes 73760 | tf_op jit(solution)/shard_map/ppermute | solution.py:16
  215.2 2.0 copy.18
  217.1 4.6 %collective-permute-start.10 = (bf16[18,18,64]{2,1,0:T(8,128)(2,1)S(1)}, bf16[18,18,64]{2,1,0:T(8,128)(2,1)S(1)}, u32[]{:S(2)}, u32[]{:S(2)}) collective-permute-start(bf16[18,18,64]{2,1,0:T(8,128)(2,1)S(1)} %get-tuple-element.58), channel_id=1, source_target_pairs={{0,4},{4,8},{8,12},{12,16},{16,20},{20,24},{24,28},{1,5},{5,9},{9,... | collective-permute-start | bytes 124424 | tf_op jit(solution)/shard_map/ppermute | solution.py:16
  221.7 2.3 collective-permute-done.10
  224.0 4.5 %concatenate.23 = bf16[18,18,2176]{2,1,0:T(8,128)(2,1)} concatenate(bf16[18,18,64]{2,1,0:T(8,128)(2,1)S(1)} %broadcast_select_fusion.6, bf16[18,18,2048]{2,1,0:T(8,128)(2,1)} %copy-done.76, bf16[18,18,64]{2,1,0:T(8,128)(2,1)S(1)} %broadcast_select_fusion.4), dimensions={2} | concatenate | bytes 2820096 | tf_op jit(solution)/shard_map/concatenate | solution.py:67
  228.5 4.4 %reshape.301 = bf16[18,18,34,64]{3,2,1,0:T(8,128)(2,1)S(1)} reshape(bf16[18,18,2176]{2,1,0:T(8,128)(2,1)} %concatenate.23) | data formatting | bytes 2820096 | tf_op jit(solution)/shard_map/reshape | solution.py:133
  232.9 13.2 %fusion.38 = (bf16[16,16,32,64]{3,2,1,0:T(8,128)(2,1)S(1)}, bf16[16,16,32,64]{3,2,1,0:T(8,128)(2,1)S(1)}, bf16[16,16,32,64]{3,2,1,0:T(8,128)(2,1)S(1)}, bf16[16,...) fusion(bf16[18,18,34,64]{3,2,1,0:T(8,128)(2,1)S(1)} %reshape.301), kind=kLoop, calls=%fused_computation.202 | loop fusion | bytes 39845888 | tf_op jit(solution)/shard_map/slice | solution.py:76
  246.1 6.6 %fusion.39 = (bf16[16,16,32,64]{3,2,1,0:T(8,128)(2,1)S(1)}, bf16[16,16,32,64]{3,2,1,0:T(8,128)(2,1)}, bf16[16,16,32,64]{3,2,1,0:T(8,128)(2,1)}, bf16[16,16,32,64...) fusion(bf16[18,18,34,64]{3,2,1,0:T(8,128)(2,1)S(1)} %reshape.301), kind=kLoop, calls=%fused_computation.203 | loop fusion | bytes 16777216 | tf_op jit(solution)/shard_map/slice | solution.py:76
  291.6 2.8 copy.20
  294.4 3.7 %reshape_reshape.10 = f32[2,8,2,8,4,512]{5,4,3,2,1,0:T(4,128)S(1)} reshape(f32[8192,64]{1,0:T(8,128)} %copy.20) | data formatting | bytes 4194304 | tf_op jit(solution)/shard_map/reshape;reshape | solution.py:41
  300.3 2.2 multiply_convert_fusion
  302.5 43.4 %all-reduce.2.cloned.1.call-done = f32[27,64,64]{2,1,0:T(8,128)} async-done(((f32[27,64,64]{2,1,0:T(8,128)}), f32[27,64,64]{2,1,0:T(8,128)}) %all-reduce.2.cloned.1.call-update) | async-done | bytes 442384 | tf_op jit(solution)/shard_map/psum | solution.py:151
  (298 shorter events, 140.7 us)
Async XLA Ops:
  7.2 338.8 %all-reduce.2.cloned.1.call-start = ((), (), s32[]{:S(2)}) async-start(), calls=%async_computation | async-start | bytes 1769472 | tf_op jit(solution)/shard_map/psum | solution.py:151
  8.0 10.3 %copy-start.85 = (s32[1,16]{1,0:T(1,128)S(1)}, s32[1,16]{1,0:T(1,128)}, u32[]{:S(2)}) copy-start(s32[1,16]{1,0:T(1,128)} %param.6) | copy-start | bytes 196
  8.0 10.8 %copy-start.83 = (bf16[27,16,64]{2,1,0:T(8,128)(2,1)S(1)}, bf16[27,16,64]{2,1,0:T(8,128)(2,1)}, u32[]{:S(2)}) copy-start(bf16[27,16,64]{2,1,0:T(8,128)(2,1)} %param.7) | copy-start | bytes 165892
  10.9 14.6 %collective-permute-start = (bf16[1,16,2048]{2,1,0:T(8,128)(2,1)S(1)}, bf16[1,16,2048]{2,1,0:T(8,128)(2,1)S(1)}, u32[]{:S(2)}, u32[]{:S(2)}) collective-permute-start(bf16[1,16,2048]{2,1,0:T(8,128)(2,1)S(1)} %get-tuple-element.67), channel_id=1, source_target_pairs={{0,16},{4,20},{8,24},{12,28},{1,17},{5,21},{9,25},{13,29},{2,18},{... | collective-permute-start | bytes 196616 | tf_op jit(solution)/shard_map/ppermute | solution.py:16
  16.9 8.6 %collective-permute-start.1 = (bf16[1,16,2048]{2,1,0:T(8,128)(2,1)S(1)}, bf16[1,16,2048]{2,1,0:T(8,128)(2,1)S(1)}, u32[]{:S(2)}, u32[]{:S(2)}) collective-permute-start(bf16[1,16,2048]{2,1,0:T(8,128)(2,1)S(1)} %get-tuple-element.68), channel_id=1, source_target_pairs={{16,0},{20,4},{24,8},{28,12},{17,1},{21,5},{25,9},{29,13},{18,2},{... | collective-permute-start | bytes 196616 | tf_op jit(solution)/shard_map/ppermute | solution.py:16
  25.5 13.1 %copy-start.80 = (bf16[27,64,64]{2,1,0:T(8,128)(2,1)}, bf16[27,64,64]{2,1,0:T(8,128)(2,1)S(1)}, u32[]{:S(2)}) copy-start(bf16[27,64,64]{2,1,0:T(8,128)(2,1)S(1)} %all_gather.3) | copy-start | bytes 663556
  25.8 7.1 %collective-permute-start.2 = (bf16[18,1,2048]{2,1,0:T(2,128)(2,1)S(1)}, bf16[18,1,2048]{2,1,0:T(2,128)(2,1)S(1)}, u32[]{:S(2)}, u32[]{:S(2)}) collective-permute-start(bf16[18,1,2048]{2,1,0:T(2,128)(2,1)S(1)} %get-tuple-element.63), channel_id=1, source_target_pairs={{0,8},{4,12},{8,16},{12,20},{16,24},{20,28},{1,9},{5,13},{9,17},{1... | collective-permute-start | bytes 221192 | tf_op jit(solution)/shard_map/ppermute | solution.py:16
  30.1 8.5 %collective-permute-start.3 = (bf16[18,1,2048]{2,1,0:T(2,128)(2,1)S(1)}, bf16[18,1,2048]{2,1,0:T(2,128)(2,1)S(1)}, u32[]{:S(2)}, u32[]{:S(2)}) collective-permute-start(bf16[18,1,2048]{2,1,0:T(2,128)(2,1)S(1)} %get-tuple-element.64), channel_id=1, source_target_pairs={{8,0},{12,4},{16,8},{20,12},{24,16},{28,20},{9,1},{13,5},{17,9},{2... | collective-permute-start | bytes 221192 | tf_op jit(solution)/shard_map/ppermute | solution.py:16
  39.8 6.6 %collective-permute-start.5 = (bf16[18,18,64]{2,1,0:T(8,128)(2,1)S(1)}, bf16[18,18,64]{2,1,0:T(8,128)(2,1)S(1)}, u32[]{:S(2)}, u32[]{:S(2)}) collective-permute-start(bf16[18,18,64]{2,1,0:T(8,128)(2,1)S(1)} %get-tuple-element.59), channel_id=1, source_target_pairs={{4,0},{8,4},{12,8},{16,12},{20,16},{24,20},{28,24},{5,1},{9,5},{13... | collective-permute-start | bytes 124424 | tf_op jit(solution)/shard_map/ppermute | solution.py:16
  41.3 7.4 %collective-permute-start.4 = (bf16[18,18,64]{2,1,0:T(8,128)(2,1)S(1)}, bf16[18,18,64]{2,1,0:T(8,128)(2,1)S(1)}, u32[]{:S(2)}, u32[]{:S(2)}) collective-permute-start(bf16[18,18,64]{2,1,0:T(8,128)(2,1)S(1)} %get-tuple-element.60), channel_id=1, source_target_pairs={{0,4},{4,8},{8,12},{12,16},{16,20},{20,24},{24,28},{1,5},{5,9},{9,... | collective-permute-start | bytes 124424 | tf_op jit(solution)/shard_map/ppermute | solution.py:16
  69.4 44.8 %copy-start.6 = (bf16[16,16,32,64]{3,2,1,0:T(8,128)(2,1)}, bf16[16,16,32,64]{3,2,1,0:T(8,128)(2,1)S(1)}, u32[]{:S(2)}) copy-start(bf16[16,16,32,64]{3,2,1,0:T(8,128)(2,1)S(1)} %get-tuple-element.33) | copy-start | bytes 3145732
  69.4 45.7 %copy-start.4 = (bf16[16,16,32,64]{3,2,1,0:T(8,128)(2,1)}, bf16[16,16,32,64]{3,2,1,0:T(8,128)(2,1)S(1)}, u32[]{:S(2)}) copy-start(bf16[16,16,32,64]{3,2,1,0:T(8,128)(2,1)S(1)} %get-tuple-element.32) | copy-start | bytes 3145732
  69.4 58.6 %copy-start.2 = (bf16[16,16,32,64]{3,2,1,0:T(8,128)(2,1)}, bf16[16,16,32,64]{3,2,1,0:T(8,128)(2,1)S(1)}, u32[]{:S(2)}) copy-start(bf16[16,16,32,64]{3,2,1,0:T(8,128)(2,1)S(1)} %get-tuple-element.31) | copy-start | bytes 3145732
  69.5 59.5 %copy-start = (bf16[16,16,32,64]{3,2,1,0:T(8,128)(2,1)}, bf16[16,16,32,64]{3,2,1,0:T(8,128)(2,1)S(1)}, u32[]{:S(2)}) copy-start(bf16[16,16,32,64]{3,2,1,0:T(8,128)(2,1)S(1)} %get-tuple-element.30) | copy-start | bytes 3145732
  69.5 7.8 %copy-start.81 = (bf16[27,64,64]{2,1,0:T(8,128)(2,1)S(1)}, bf16[27,64,64]{2,1,0:T(8,128)(2,1)}, u32[]{:S(2)}) copy-start(bf16[27,64,64]{2,1,0:T(8,128)(2,1)} %copy-done.80) | copy-start | bytes 663556
  77.2 11.3 %copy-start.40 = (bf16[16,16,32,64]{3,2,1,0:T(8,128)(2,1)}, bf16[16,16,32,64]{3,2,1,0:T(8,128)(2,1)S(1)}, u32[]{:S(2)}) copy-start(bf16[16,16,32,64]{3,2,1,0:T(8,128)(2,1)S(1)} %get-tuple-element.50) | copy-start | bytes 3145732
  77.2 12.2 %copy-start.38 = (bf16[16,16,32,64]{3,2,1,0:T(8,128)(2,1)}, bf16[16,16,32,64]{3,2,1,0:T(8,128)(2,1)S(1)}, u32[]{:S(2)}) copy-start(bf16[16,16,32,64]{3,2,1,0:T(8,128)(2,1)S(1)} %get-tuple-element.49) | copy-start | bytes 3145732
  77.2 4.0 %copy-start.50 = (bf16[16,16,32,64]{3,2,1,0:T(8,128)(2,1)S(1)}, bf16[16,16,32,64]{3,2,1,0:T(8,128)(2,1)}, u32[]{:S(2)}) copy-start(bf16[16,16,32,64]{3,2,1,0:T(8,128)(2,1)} %get-tuple-element.55) | copy-start | bytes 3145732
  132.7 3.8 %copy-start.78 = (bf16[1,16,8,8,512]{4,3,2,1,0:T(8,128)(2,1)S(1)}, bf16[1,16,8,8,512]{4,3,2,1,0:T(8,128)(2,1)}, u32[]{:S(2)}) copy-start(bf16[1,16,8,8,512]{4,3,2,1,0:T(8,128)(2,1)} %param.5) | copy-start | bytes 3145732
  144.3 2.5 copy-start.51
  183.4 7.7 %copy-start.3 = (bf16[16,16,32,64]{3,2,1,0:T(8,128)(2,1)S(1)}, bf16[16,16,32,64]{3,2,1,0:T(8,128)(2,1)}, u32[]{:S(2)}) copy-start(bf16[16,16,32,64]{3,2,1,0:T(8,128)(2,1)} %copy-done.2) | copy-start | bytes 3145732
  184.2 18.5 %copy-start.1 = (bf16[16,16,32,64]{3,2,1,0:T(8,128)(2,1)S(1)}, bf16[16,16,32,64]{3,2,1,0:T(8,128)(2,1)}, u32[]{:S(2)}) copy-start(bf16[16,16,32,64]{3,2,1,0:T(8,128)(2,1)} %copy-done) | copy-start | bytes 3145732
  184.2 9.0 %collective-permute-start.6 = (bf16[1,16,2048]{2,1,0:T(8,128)(2,1)S(1)}, bf16[1,16,2048]{2,1,0:T(8,128)(2,1)S(1)}, u32[]{:S(2)}, u32[]{:S(2)}) collective-permute-start(bf16[1,16,2048]{2,1,0:T(8,128)(2,1)S(1)} %get-tuple-element.65), channel_id=1, source_target_pairs={{0,16},{4,20},{8,24},{12,28},{1,17},{5,21},{9,25},{13,29},{2,18},{... | collective-permute-start | bytes 196616 | tf_op jit(solution)/shard_map/ppermute | solution.py:16
  191.8 7.1 %collective-permute-start.7 = (bf16[1,16,2048]{2,1,0:T(8,128)(2,1)S(1)}, bf16[1,16,2048]{2,1,0:T(8,128)(2,1)S(1)}, u32[]{:S(2)}, u32[]{:S(2)}) collective-permute-start(bf16[1,16,2048]{2,1,0:T(8,128)(2,1)S(1)} %get-tuple-element.66), channel_id=1, source_target_pairs={{16,0},{20,4},{24,8},{28,12},{17,1},{21,5},{25,9},{29,13},{18,2},{... | collective-permute-start | bytes 196616 | tf_op jit(solution)/shard_map/ppermute | solution.py:16
  199.1 6.1 %collective-permute-start.8 = (bf16[18,1,2048]{2,1,0:T(2,128)(2,1)S(1)}, bf16[18,1,2048]{2,1,0:T(2,128)(2,1)S(1)}, u32[]{:S(2)}, u32[]{:S(2)}) collective-permute-start(bf16[18,1,2048]{2,1,0:T(2,128)(2,1)S(1)} %get-tuple-element.61), channel_id=1, source_target_pairs={{0,8},{4,12},{8,16},{12,20},{16,24},{20,28},{1,9},{5,13},{9,17},{1... | collective-permute-start | bytes 221192 | tf_op jit(solution)/shard_map/ppermute | solution.py:16
  203.4 7.0 %collective-permute-start.9 = (bf16[18,1,2048]{2,1,0:T(2,128)(2,1)S(1)}, bf16[18,1,2048]{2,1,0:T(2,128)(2,1)S(1)}, u32[]{:S(2)}, u32[]{:S(2)}) collective-permute-start(bf16[18,1,2048]{2,1,0:T(2,128)(2,1)S(1)} %get-tuple-element.62), channel_id=1, source_target_pairs={{8,0},{12,4},{16,8},{20,12},{24,16},{28,20},{9,1},{13,5},{17,9},{2... | collective-permute-start | bytes 221192 | tf_op jit(solution)/shard_map/ppermute | solution.py:16
  210.6 4.6 %copy-start.53 = (f32[2,8,2,8,4,512]{5,4,3,2,1,0:T(4,128)S(1)}, f32[2,8,2,8,4,512]{5,4,3,2,1,0:T(4,128)}, u32[]{:S(2)}) copy-start(f32[2,8,2,8,4,512]{5,4,3,2,1,0:T(4,128)} %copy-done.52) | copy-start | bytes 6291460
  212.9 8.8 %collective-permute-start.11 = (bf16[18,18,64]{2,1,0:T(8,128)(2,1)S(1)}, bf16[18,18,64]{2,1,0:T(8,128)(2,1)S(1)}, u32[]{:S(2)}, u32[]{:S(2)}) collective-permute-start(bf16[18,18,64]{2,1,0:T(8,128)(2,1)S(1)} %get-tuple-element.57), channel_id=1, source_target_pairs={{4,0},{8,4},{12,8},{16,12},{20,16},{24,20},{28,24},{5,1},{9,5},{13... | collective-permute-start | bytes 124424 | tf_op jit(solution)/shard_map/ppermute | solution.py:16
  217.1 6.9 %collective-permute-start.10 = (bf16[18,18,64]{2,1,0:T(8,128)(2,1)S(1)}, bf16[18,18,64]{2,1,0:T(8,128)(2,1)S(1)}, u32[]{:S(2)}, u32[]{:S(2)}) collective-permute-start(bf16[18,18,64]{2,1,0:T(8,128)(2,1)S(1)} %get-tuple-element.58), channel_id=1, source_target_pairs={{0,4},{4,8},{8,12},{12,16},{16,20},{20,24},{24,28},{1,5},{5,9},{9,... | collective-permute-start | bytes 124424 | tf_op jit(solution)/shard_map/ppermute | solution.py:16
  246.1 6.6 %copy-start.82 = (bf16[27,64,64]{1,2,0:T(8,128)(2,1)S(1)}, bf16[27,64,64]{1,2,0:T(8,128)(2,1)}, u32[]{:S(2)}) copy-start(bf16[27,64,64]{1,2,0:T(8,128)(2,1)} %reverse_bitcast_fusion) | copy-start | bytes 663556
  298.1 2.2 copy-start.79
  298.1 2.2 copy-start.84
  (67 other events, 106.4 us)
Sparse Core Ops, SparseCore 0:
  217.3 128.6 all-reduce.1
where the time goes:
time: 359 us; the launch traced here: 355 us
  local copies, waits for them, and re-layouts  135 us (38%)
  matrix products  83.5 us (23%)
  waiting for transfers between devices  66.9 us (19%)
  starting transfers between devices  36.7 us (10%)
  between operations  15.4 us (4%)
  other arithmetic  10.8 us (3%)
  blocking collectives  6.74 us (2%)
    dot_general x54, matrix products, correlate(): jnp.dot(tap_rows(padded, tap_index, shape_out), taps[tap_index], preferre...  62.2 us
    unnamed x172, local copies, waits for them, and re-layouts  51.5 us
    psum x1, waiting for transfers between devices, local(): grad_whole = lax.psum(grad_term, ('space', 'fsdp'))  43.4 us
    slice x4, local copies, waits for them, and re-layouts, tap_rows(): padded[shift_x:shift_x + size_x, shift_y:shift_y + size_y, shift_z:shift_...  40.7 us
    ppermute x12, starting transfers between devices, from_behind(): return lax.ppermute(shard, axis, pairs)  36.7 us
    ppermute x12, waiting for transfers between devices, from_behind(): return lax.ppermute(shard, axis, pairs)  23.5 us
    dot_general x27, matrix products, weight_terms(): lax.dot_general(rows_in, grad_rows, (((0,), (0,)), ((), ())), preferred_e...  21.3 us
    another operation x3, local copies, waits for them, and re-layouts, to_bricks(): volume.reshape(BRICK_X, edge_cells, BRICK_Y, edge_cells, BRICK_Z, edge_ce...  9.47 us
  transfers between devices with their start and end apart: 13, of which 9 were waited for; matrix products, arithmetic and copies ran while one was open for 19% of the time, Pallas kernels for 0%

commit v1 on v0

v1 whole, which is shorter than its diff:
```python
import math

import jax
import jax.numpy as jnp
from jax import lax
from jax.sharding import PartitionSpec as P

BRICK_X = 2
BRICK_Y = 2
BRICK_Z = 4
PAIR = 2
DEPTH = 2

CONV_DIMS = ("NDHWC", "DHWIO", "NDHWC")


def from_behind(shard, axis, by):
    peers = lax.axis_size(axis)
    pairs = [(i, i + by) for i in range(peers) if 0 <= i + by < peers]
    return lax.ppermute(shard, axis, pairs)


def grid_shape(number):
    factors = [1, 1, 1]
    places = 0
    while number % 2 == 0:
        factors[places % 3] = factors[places % 3] * 2
        number = number // 2
        places = places + 1
    factors[0] = factors[0] * number
    return factors


def to_volume(bricks, edge_cells, lanes):
    per_brick = edge_cells // PAIR
    blocks = bricks.reshape(
        BRICK_X, BRICK_Y, BRICK_Z, edge_cells, edge_cells, per_brick, lanes
    )
    blocks = blocks.transpose(0, 3, 1, 4, 2, 5, 6)
    return blocks.reshape(
        BRICK_X * edge_cells, BRICK_Y * edge_cells, BRICK_Z * per_brick, lanes
    )


def to_bricks(volume, edge_cells, lanes):
    per_brick = edge_cells // PAIR
    blocks = volume.reshape(
        BRICK_X, edge_cells, BRICK_Y, edge_cells, BRICK_Z, per_brick, lanes
    )
    blocks = blocks.transpose(0, 2, 4, 1, 3, 5, 6)
    return blocks.reshape(
        BRICK_X * BRICK_Y * BRICK_Z, edge_cells, edge_cells, per_brick * lanes
    )


def neighbour_plane(portion, offset, present):
    arrived = from_behind(portion, "space", offset)
    return jnp.where(present, arrived, jnp.zeros_like(arrived))


def extend(volume, grid_dims, places, widths):
    strides = (grid_dims[1] * grid_dims[2], grid_dims[2], 1)
    for axis_pos in range(3):
        axis = axis_pos + 1
        extent = volume.shape[axis]
        width = widths[axis_pos]
        last_layer = lax.slice_in_dim(volume, extent - width, extent, axis=axis)
        first_layer = lax.slice_in_dim(volume, 0, width, axis=axis)
        from_below = neighbour_plane(last_layer, strides[axis_pos], places[axis_pos] > 0)
        from_above = neighbour_plane(
            first_layer, -strides[axis_pos], places[axis_pos] < grid_dims[axis_pos] - 1
        )
        volume = jnp.concatenate([from_below, volume, from_above], axis=axis)
    return volume


def super_kernel(weight_full, channels):
    taps = weight_full.reshape(3, 3, 3, channels, channels)
    zero = jnp.zeros((3, 3, channels, channels), weight_full.dtype)
    rows = []
    for dz in range(3):
        row = []
        for hi in range(PAIR):
            col = []
            for ho in range(PAIR):
                c = 2 * dz - 1 + hi - ho
                col.append(taps[:, :, c] if 0 <= c < 3 else zero)
            row.append(jnp.concatenate(col, axis=-1))
        rows.append(jnp.concatenate(row, axis=-2))
    return jnp.stack(rows, axis=2)


def fold_kernel_grad(grad_sup, channels):
    taps = [None, None, None]
    for dz in range(3):
        for hi in range(PAIR):
            for ho in range(PAIR):
                c = 2 * dz - 1 + hi - ho
                if 0 <= c < 3:
                    block = grad_sup[
                        :, :, dz, hi * channels : (hi + 1) * channels, ho * channels : (ho + 1) * channels
                    ]
                    taps[c] = block if taps[c] is None else taps[c] + block
    return jnp.stack(taps, axis=2).reshape(27, channels, channels)


def conv(volume, kernel):
    return lax.conv_general_dilated(
        volume[None],
        kernel,
        (1, 1, 1),
        "VALID",
        dimension_numbers=CONV_DIMS,
        preferred_element_type=jnp.float32,
    )[0]


def kernel_grad(inputs, grads):
    out = lax.conv_general_dilated(
        inputs[None],
        grads[None],
        (1, 1, 1),
        "VALID",
        dimension_numbers=("CDHWN", "IDHWO", "NDHWC"),
        preferred_element_type=jnp.float32,
    )
    return out.transpose(1, 2, 3, 0, 4)


def local(features, cotangent, tissue, weight):
    edge_cells = features.shape[2]
    channels = weight.shape[2]
    lanes = PAIR * channels
    grid_dims = grid_shape(lax.axis_size("space"))
    index_now = lax.axis_index("space")
    places = (
        index_now // (grid_dims[1] * grid_dims[2]),
        index_now // grid_dims[2] % grid_dims[1],
        index_now % grid_dims[2],
    )
    weight_full = lax.all_gather(weight, "fsdp", axis=1, tiled=True)
    k_fwd = super_kernel(weight_full, channels)
    k_back = jnp.flip(k_fwd, (0, 1, 2)).transpose(0, 1, 2, 4, 3)

    present = tissue[0][:, None, None, None] > 0
    inputs = features[0]
    incoming = cotangent[0]
    masked = jnp.where(present, inputs, jnp.zeros_like(inputs))
    masked_cot = jnp.where(present, incoming, jnp.zeros_like(incoming))

    both = jnp.stack(
        [to_volume(masked, edge_cells, lanes), to_volume(masked_cot, edge_cells, lanes)]
    )
    grown = extend(both, grid_dims, places, (DEPTH, DEPTH, 1))
    grown = jnp.pad(grown, ((0, 0), (0, 0), (0, 0), (1, 1), (0, 0)))
    padded_in = grown[0]
    cot_ext = grown[1, 1:-1, 1:-1, 1:-1]

    pre_ext = conv(padded_in, k_fwd)
    gate_ext = jax.nn.sigmoid(pre_ext)
    slope_ext = gate_ext * (1.0 + pre_ext * (1.0 - gate_ext))
    grad_ext = (cot_ext.astype(jnp.float32) * slope_ext).astype(jnp.bfloat16)

    tissue_mask = tissue[0].astype(jnp.float32)[:, None, None, None]
    pre = to_bricks(pre_ext[1:-1, 1:-1, 1:-1], edge_cells, lanes)
    gate_val = to_bricks(gate_ext[1:-1, 1:-1, 1:-1], edge_cells, lanes)
    activations = (tissue_mask * (inputs.astype(jnp.float32) + pre * gate_val)).astype(
        jnp.bfloat16
    )

    back = to_bricks(conv(grad_ext, k_back), edge_cells, lanes)
    input_grad = (tissue_mask * (incoming.astype(jnp.float32) + back)).astype(jnp.bfloat16)

    total_cells = (
        lax.axis_size("space") * lax.axis_size("fsdp") * BRICK_X * BRICK_Y * BRICK_Z * edge_cells**3
    )
    grad_sup = kernel_grad(padded_in[1:-1, 1:-1, 1:-1], grad_ext[1:-1, 1:-1, 1:-1])
    grad_term = fold_kernel_grad(grad_sup, channels) / math.sqrt(total_cells)
    grad_part = lax.psum_scatter(grad_term, "fsdp", scatter_dimension=1, tiled=True)
    grad_part = lax.psum(grad_part, "space")
    return (activations[None], input_grad[None], grad_part)


def solution(mesh):
    return jax.shard_map(
        local,
        mesh=mesh,
        in_specs=(
            P("fsdp", "space", None, None, None),
            P("fsdp", "space", None, None, None),
            P("fsdp", "space"),
            P(None, "fsdp", None),
        ),
        out_specs=(
            P("fsdp", "space", None, None, None),
            P("fsdp", "space", None, None, None),
            P(None, "fsdp", None),
        ),
        check_vma=False,
    )
```

time: 359 us -> 296 us (0.82)
  local copies, waits for them, and re-layouts: 135 us -> 51 us
  waiting for transfers between devices: 66.9 us -> 101 us
  other arithmetic: 10.8 us -> 33.8 us
  matrix products: 83.5 us -> 62.5 us
  starting transfers between devices: 36.7 us -> 20.3 us
    dot_general x81 -> x0, matrix products: 83.5 us -> none  [the longest x54 62.2 us: correlate(): jnp.dot(tap_rows(padded, tap_index, shape_out), taps[tap_index], preferre...]
    unnamed x172 -> x40, local copies, waits for them, and re-layouts: 51.5 us -> 6.21 us
    slice x8 -> x1, local copies, waits for them, and re-layouts: 40.9 us -> 0.74 us  [local(): padded_in = grown[0]]
    transpose x0 -> x1, matrix products: none -> 32.2 us  [kernel_grad(): return out.transpose(1, 2, 3, 0, 4)]
    conv_general_dilated x0 -> x2, matrix products: none -> 30.3 us  [conv(): lax.conv_general_dilated(volume[None], kernel, (1, 1, 1), 'VALID', dimens...]
    psum x1, waiting for transfers between devices: 43.4 us -> 70 us  [local(): grad_part = lax.psum(grad_part, 'space')]
    conv_general_dilated x0 -> x9, local copies, waits for them, and re-layouts: none -> 20.1 us  [conv(): lax.conv_general_dilated(volume[None], kernel, (1, 1, 1), 'VALID', dimens...]
    ppermute x12 -> x6, starting transfers between devices: 36.7 us -> 20 us  [from_behind(): return lax.ppermute(shard, axis, pairs)]
  transfers between devices with their start and end apart: 13 -> 8, of which waited for: 9 -> 7; matrix products, arithmetic and copies ran while one was open for 19% -> 8% of each run, Pallas kernels for 0% -> 0%
where the time goes in v1:
time: 296 us; the launch traced here: 291 us
  waiting for transfers between devices  101 us (34%)
  matrix products  62.5 us (21%)
  local copies, waits for them, and re-layouts  51 us (17%)
  other arithmetic  33.8 us (11%)
  starting transfers between devices  20.3 us (7%)
  between operations  14.9 us (5%)
  blocking collectives  7.7 us (3%)
    psum x1, waiting for transfers between devices, local(): grad_part = lax.psum(grad_part, 'space')  70 us
    transpose x1, matrix products, kernel_grad(): return out.transpose(1, 2, 3, 0, 4)  32.2 us
    conv_general_dilated x2, matrix products, conv(): lax.conv_general_dilated(volume[None], kernel, (1, 1, 1), 'VALID', dimens...  30.3 us
    ppermute x6, waiting for transfers between devices, from_behind(): return lax.ppermute(shard, axis, pairs)  23.2 us
    conv_general_dilated x9, local copies, waits for them, and re-layouts, conv(): lax.conv_general_dilated(volume[None], kernel, (1, 1, 1), 'VALID', dimens...  20.1 us
    ppermute x6, starting transfers between devices, from_behind(): return lax.ppermute(shard, axis, pairs)  20 us
    mul x2, local copies, waits for them, and re-layouts, local(): slope_ext = gate_ext * (1.0 + pre_ext * (1.0 - gate_ext))  11.3 us
    all_gather x1, blocking collectives, local(): weight_full = lax.all_gather(weight, 'fsdp', axis=1, tiled=True)  7.7 us
  transfers between devices with their start and end apart: 8, of which 7 were waited for; matrix products, arithmetic and copies ran while one was open for 8% of the time, Pallas kernels for 0%

profile of v1, /device:TPU:0, one launch (start us, length us, event | category | flops | bytes accessed | tf_op | source)
XLA Modules:
  0.0 291.2 jit_solution(907447351510930595)
XLA Ops:
  8.0 2.7 copy_select_fusion.1
  12.0 6.7 %collective-permute-start = (bf16[2,2,16,16,128]{4,3,2,1,0:T(8,128)(2,1)S(1)}, bf16[2,2,16,16,128]{4,3,2,1,0:T(8,128)(2,1)S(1)}, u32[]{:S(2)}, u32[]{:S(2)}) collective-permute-start(bf16[2,2,16,16,128]{4,3,2,1,0:T(8,128)(2,1)S(1)} %get-tuple-element.11), channel_id=1, source_target_pairs={{0,16},{4,20},{8,24},{12,28},{1,17},{5,21},{9,25},{13,29},{2,18},{... | collective-permute-start | bytes 786440 | tf_op jit(solution)/shard_map/ppermute | solution.py:20
  18.7 7.7 %all_gather.3 = bf16[27,64,64]{2,1,0:T(8,128)(2,1)S(1)} all-gather(bf16[27,16,64]{2,1,0:T(8,128)(2,1)S(1)} %copy-done.14), channel_id=1, replica_groups=mesh['space'=8,'fsdp'=4] {'fsdp'}, dimensions={1}, use_global_device_ids=true | all-gather | bytes 276480 | tf_op jit(solution)/shard_map/all_gather | solution.py:141
  26.4 1.7 collective-permute-done.1
  30.6 4.8 %collective-permute-start.2 = (bf16[2,20,2,16,128]{4,3,2,1,0:T(8,128)(2,1)S(1)}, bf16[2,20,2,16,128]{4,3,2,1,0:T(8,128)(2,1)S(1)}, u32[]{:S(2)}, u32[]{:S(2)}) collective-permute-start(bf16[2,20,2,16,128]{4,3,2,1,0:T(8,128)(2,1)S(1)} %get-tuple-element.9), channel_id=1, source_target_pairs={{0,8},{4,12},{8,16},{12,20},{16,24},{20,28},{1,9},{5,13},{9,17},{1... | collective-permute-start | bytes 983048 | tf_op jit(solution)/shard_map/ppermute | solution.py:20
  35.7 5.6 %collective-permute-done.3 = bf16[2,20,2,16,128]{4,3,2,1,0:T(8,128)(2,1)S(1)} collective-permute-done((bf16[2,20,2,16,128]{4,3,2,1,0:T(8,128)(2,1)S(1)}, bf16[2,20,2,16,128]{4,3,2,1,0:T(8,128)(2,1)S(1)}, u32[]{:S(2)}, u32[]{:S(2)}) %collective-permute-start.3) | collective-permute-done | bytes 327712 | tf_op jit(solution)/shard_map/ppermute | solution.py:20
  42.5 1.9 pad_maximum_fusion.7
  46.2 4.7 %collective-permute-start.4 = (bf16[2,20,20,1,128]{4,3,2,1,0:T(2,128)(2,1)S(1)}, bf16[2,20,20,1,128]{4,3,2,1,0:T(2,128)(2,1)S(1)}, u32[]{:S(2)}, u32[]{:S(2)}) collective-permute-start(bf16[2,20,20,1,128]{4,3,2,1,0:T(2,128)(2,1)S(1)} %get-tuple-element.7), channel_id=1, source_target_pairs={{0,4},{4,8},{8,12},{12,16},{16,20},{20,24},{24,28},{1,5},{5,9},{9,... | collective-permute-start | bytes 614408 | tf_op jit(solution)/shard_map/ppermute | solution.py:20
  50.9 6.3 %collective-permute-done.5 = bf16[2,20,20,1,128]{4,3,2,1,0:T(2,128)(2,1)S(1)} collective-permute-done((bf16[2,20,20,1,128]{4,3,2,1,0:T(2,128)(2,1)S(1)}, bf16[2,20,20,1,128]{4,3,2,1,0:T(2,128)(2,1)S(1)}, u32[]{:S(2)}, u32[]{:S(2)}) %collective-permute-start.5) | collective-permute-done | bytes 204832 | tf_op jit(solution)/shard_map/ppermute | solution.py:20
  57.7 8.5 %collective-permute-done.4 = bf16[2,20,20,1,128]{4,3,2,1,0:T(2,128)(2,1)S(1)} collective-permute-done((bf16[2,20,20,1,128]{4,3,2,1,0:T(2,128)(2,1)S(1)}, bf16[2,20,20,1,128]{4,3,2,1,0:T(2,128)(2,1)S(1)}, u32[]{:S(2)}, u32[]{:S(2)}) %collective-permute-start.4) | collective-permute-done | bytes 204832 | tf_op jit(solution)/shard_map/ppermute | solution.py:20
  66.6 5.9 %pad_maximum_fusion = bf16[2,20,20,18,128]{4,3,2,1,0:T(8,128)(2,1)S(1)} fusion(bf16[2,20,20,1,128]{4,3,2,1,0:T(2,128)(2,1)S(1)} %broadcast_select_fusion.1, bf16[2,20,2,16,128]{4,3,2,1,0:T(8,128)(2,1)S(1)} %broadcast_select_fusion.3, bf16[2,2,16,16,128]{4,3,2,1,0:T(8,128)(2,1)S(1)} %broadcast_select_fusion.5, bf16[1,16,16,16,128]{4,3,2,1,0:T(8,128)(2,1)S(1)} %bitcast.89, ...), kind=kLoop, calls=%fused_computation.6 | loop fusion | flops 29491200 | bytes 7372800 | tf_op jit(solution)/shard_map/concatenate | solution.py:73
  72.5 3.0 %fusion.29 = (bf16[20,20,20,128]{3,2,1,0:T(8,128)(2,1)}, bf16[20,20,1,20,128]{4,3,1,0,2:T(8,128)(2,1)S(1)}) fusion(bf16[2,20,20,18,128]{4,3,2,1,0:T(8,128)(2,1)S(1)} %pad_maximum_fusion), kind=kLoop, calls=%fused_computation.39 | loop fusion | bytes 7782400 | tf_op jit(solution)/shard_map/squeeze | solution.py:156
  77.5 17.0 %add_multiply_fusion = (f32[18,18,8,3,128]{4,2,3,1,0:T(8,128)}, f32[18,18,8,3,128]{4,2,3,1,0:T(8,128)S(1)}) fusion(bf16[3,3,1,128,128]{4,3,2,1,0:T(8,128)(2,1)S(1)} %get-tuple-element.21, bf16[3,3,1,128,128]{4,3,2,1,0:T(8,128)(2,1)S(1)} %get-tuple-element.20, bf16[3,3,1,128,128]{4,3,2,1,0:T(8,128)(2,1)S(1)} %get-tuple-element.19, ...), kind=kOutput, calls=%fused_computation.17 | convolution fusion | flops 6900842496 | bytes 12738584 | tf_op jit(solution)/shard_map/conv_general_dilated | solution.py:108
  94.4 4.0 %copy.40 = f32[18,18,8,3,128]{4,3,2,1,0:T(4,128)} copy(f32[18,18,8,3,128]{4,2,3,1,0:T(8,128)S(1)} %get-tuple-element.27) | data formatting | bytes 7962624 | tf_op jit(solution)/shard_map/conv_general_dilated | solution.py:108
  98.4 7.3 %reshape.72 = f32[18,18,1,24,128]{4,3,1,0,2:T(8,128)} reshape(f32[18,18,8,3,128]{4,3,2,1,0:T(4,128)} %copy.40) | data formatting | bytes 7962624 | tf_op jit(solution)/shard_map/conv_general_dilated | solution.py:108
  105.7 4.5 %slice_bitcast_fusion.1 = f32[18,18,18,128]{3,2,1,0:T(8,128)} fusion(f32[18,18,1,24,128]{4,3,1,0,2:T(8,128)} %reshape.72), kind=kLoop, calls=%fused_computation.16 | loop fusion | bytes 5971968 | tf_op jit(solution)/shard_map/squeeze | solution.py:108
  110.2 3.0 %add_divide_fusion = f32[18,18,18,128]{3,2,1,0:T(8,128)} fusion(f32[18,18,1,24,128]{4,3,1,0,2:T(8,128)S(1)} %copy-done.1), kind=kLoop, calls=%fused_computation.18 | loop fusion | flops 2239488 | bytes 5971968 | tf_op jit(solution)/shard_map/div | solution.py:160
  113.2 3.9 %convert_bitcast_fusion = f32[18,18,18,128]{3,2,1,0:T(8,128)} fusion(bf16[2,20,20,18,128]{4,3,2,1,0:T(8,128)(2,1)} %copy-done), kind=kLoop, calls=%fused_computation.4 | loop fusion | flops 746496 | bytes 4478976 | tf_op jit(solution)/shard_map/convert_element_type | solution.py:162
  117.1 4.0 %copy.42 = f32[18,18,8,3,128]{4,3,2,1,0:T(4,128)} copy(f32[18,18,8,3,128]{4,2,3,1,0:T(8,128)S(1)} %copy-done.9) | data formatting | bytes 7962624 | tf_op jit(solution)/shard_map/mul | solution.py:161
  121.0 7.3 %reshape.81 = f32[18,18,1,24,128]{4,3,1,0,2:T(8,128)} reshape(f32[18,18,8,3,128]{4,3,2,1,0:T(4,128)} %copy.42) | data formatting | bytes 7962624 | tf_op jit(solution)/shard_map/mul | solution.py:161
  128.3 3.2 %fusion.22 = bf16[18,18,1,18,128]{4,3,1,0,2:T(8,128)(2,1)S(1)} fusion(f32[18,18,1,24,128]{4,3,1,0,2:T(8,128)} %reshape.81, bf16[2,20,20,18,128]{4,3,2,1,0:T(8,128)(2,1)} %copy-done), kind=kLoop, calls=%fused_computation.33 | loop fusion | flops 2239488 | bytes 5971968 | tf_op jit(solution)/shard_map/convert_element_type | solution.py:162
  131.5 1.6 pad.11
  133.1 5.5 %reshape.75 = bf16[18,18,1,8,3,128]{5,4,3,1,0,2:T(4,128)(2,1)S(1)} reshape(bf16[18,18,1,24,128]{4,3,1,0,2:T(8,128)(2,1)} %pad.11) | data formatting | bytes 3981312 | tf_op jit(solution)/shard_map/conv_general_dilated | solution.py:108
  140.3 1.5 slice.102
  144.1 4.3 %fusion.31 = (bf16[1,16,16,16,128]{4,3,2,1,0:T(8,128)(2,1)S(1)}, f32[16,16,16,128]{3,2,1,0:T(8,128)}) fusion(f32[18,18,18,128]{3,2,1,0:T(8,128)S(1)} %copy-done.2, f32[18,18,18,128]{3,2,1,0:T(8,128)S(1)} %copy-done.3, f32[18,18,18,128]{3,2,1,0:T(8,128)} %convert_bitcast_fusion), kind=kLoop, calls=%fused_computation.41 | loop fusion | flops 3670016 | bytes 9437184 | tf_op jit(solution)/shard_map/broadcast_in_dim | solution.py:121
  148.4 32.2 %fusion.17 = f32[3,3,3,128,128]{4,3,2,1,0:T(8,128)S(1)} fusion(bf16[1,18,18,18,128]{4,3,2,1,0:T(8,128)(2,1)S(1)} %slice_bitcast_fusion.2, bf16[1,16,16,16,128]{4,3,2,1,0:T(8,128)(2,1)S(1)} %get-tuple-element.3), kind=kOutput, calls=%fused_computation.25 | convolution fusion | flops 3623878656 | bytes 4311040 | tf_op jit(solution)/shard_map/transpose | solution.py:127
  182.9 13.3 %fusion.25 = f32[16,16,8,3,128]{4,2,3,1,0:T(8,128)S(1)} fusion(bf16[18,18,1,7,2,128]{5,3,4,1,0,2:T(8,128)(2,1)S(1)} %copy-done.10, bf16[18,18,1,8,3,128]{5,3,4,1,0,2:T(8,128)(2,1)S(1)} %copy-done.7, pred[8,3]{0,1:T(4,128)(4,1)S(1)} %copy-done.17, bf16[3,3,1,128,128]{4,3,2,1,0:T(8,128)(2,1)} %copy-done.13, bf16[3,3,1,128,128]{4,3,2,1,0:T(8,128)(2,1)} %copy-done.12, ...), kind=kOutput, calls=%fused_computation.37 | convolution fusion | flops 5447442432 | bytes 7182360 | tf_op jit(solution)/shard_map/conv_general_dilated | solution.py:108
  198.4 2.0 copy.41
  200.4 7.6 %reduce-scatter.2.cloned.1.call-done = f32[27,16,64]{2,1,0:T(8,128)} async-done(((f32[27,64,64]{2,1,0:T(8,128)}), f32[27,16,64]{2,1,0:T(8,128)}) %reduce-scatter.2.cloned.1.call-update) | async-done | bytes 110608 | tf_op jit(solution)/shard_map/reduce_scatter | solution.py:179
  208.1 4.2 %multiply_convert_fusion = (bf16[1,16,8,8,512]{4,3,2,1,0:T(8,128)(2,1)}, bf16[1,16,8,8,512]{4,3,2,1,0:T(8,128)(2,1)}) fusion(f32[1,16,8,8,512]{4,3,2,1,0:T(8,128)S(1)} %bitcast.94, bf16[1,16,8,8,512]{4,3,2,1,0:T(8,128)(2,1)} %param.5, f32[16]{0:T(128)S(1)} %copy-done.15, f32[1,16,8,8,512]{4,3,2,1,0:T(8,128)} %bitcast.95, ...), kind=kLoop, calls=%fused_computation.29 | loop fusion | flops 4194304 | bytes 8388672 | tf_op jit(solution)/shard_map/convert_element_type | solution.py:172
  212.3 70.0 %all-reduce.7.cloned.1.call-done = f32[27,16,64]{2,1,0:T(8,128)} async-done(((f32[27,16,64]{2,1,0:T(8,128)}), f32[27,16,64]{2,1,0:T(8,128)}) %all-reduce.7.cloned.1.call-update) | async-done | bytes 110608 | tf_op jit(solution)/shard_map/psum | solution.py:180
  282.2 1.6 copy.60
  (71 shorter events, 19.0 us)
Async XLA Ops:
  7.2 11.5 %copy-start.14 = (bf16[27,16,64]{2,1,0:T(8,128)(2,1)S(1)}, bf16[27,16,64]{2,1,0:T(8,128)(2,1)}, u32[]{:S(2)}) copy-start(bf16[27,16,64]{2,1,0:T(8,128)(2,1)} %param.7) | copy-start | bytes 165892
  7.2 200.8 %reduce-scatter.2.cloned.1.call-start = ((), (), s32[]{:S(2)}) async-start(), calls=%async_computation.1 | async-start | bytes 1105920 | tf_op jit(solution)/shard_map/reduce_scatter | solution.py:179
  10.7 17.4 %collective-permute-start.1 = (bf16[2,2,16,16,128]{4,3,2,1,0:T(8,128)(2,1)S(1)}, bf16[2,2,16,16,128]{4,3,2,1,0:T(8,128)(2,1)}, u32[]{:S(2)}, u32[]{:S(2)}) collective-permute-start(bf16[2,2,16,16,128]{4,3,2,1,0:T(8,128)(2,1)S(1)} %get-tuple-element.12), channel_id=1, source_target_pairs={{16,0},{20,4},{24,8},{28,12},{17,1},{21,5},{25,9},{29,13},{18,2},{... | collective-permute-start | bytes 786440 | tf_op jit(solution)/shard_map/ppermute | solution.py:20
  12.0 17.0 %collective-permute-start = (bf16[2,2,16,16,128]{4,3,2,1,0:T(8,128)(2,1)S(1)}, bf16[2,2,16,16,128]{4,3,2,1,0:T(8,128)(2,1)S(1)}, u32[]{:S(2)}, u32[]{:S(2)}) collective-permute-start(bf16[2,2,16,16,128]{4,3,2,1,0:T(8,128)(2,1)S(1)} %get-tuple-element.11), channel_id=1, source_target_pairs={{0,16},{4,20},{8,24},{12,28},{1,17},{5,21},{9,25},{13,29},{2,18},{... | collective-permute-start | bytes 786440 | tf_op jit(solution)/shard_map/ppermute | solution.py:20
  29.2 16.5 %copy-start.16 = (s32[1,16]{1,0:T(1,128)S(1)}, s32[1,16]{1,0:T(1,128)}, u32[]{:S(2)}) copy-start(s32[1,16]{1,0:T(1,128)} %param.6) | copy-start | bytes 196
  29.2 12.0 %collective-permute-start.3 = (bf16[2,20,2,16,128]{4,3,2,1,0:T(8,128)(2,1)S(1)}, bf16[2,20,2,16,128]{4,3,2,1,0:T(8,128)(2,1)S(1)}, u32[]{:S(2)}, u32[]{:S(2)}) collective-permute-start(bf16[2,20,2,16,128]{4,3,2,1,0:T(8,128)(2,1)S(1)} %get-tuple-element.10), channel_id=1, source_target_pairs={{8,0},{12,4},{16,8},{20,12},{24,16},{28,20},{9,1},{13,5},{17,9},{2... | collective-permute-start | bytes 983048 | tf_op jit(solution)/shard_map/ppermute | solution.py:20
  30.6 11.9 %collective-permute-start.2 = (bf16[2,20,2,16,128]{4,3,2,1,0:T(8,128)(2,1)S(1)}, bf16[2,20,2,16,128]{4,3,2,1,0:T(8,128)(2,1)S(1)}, u32[]{:S(2)}, u32[]{:S(2)}) collective-permute-start(bf16[2,20,2,16,128]{4,3,2,1,0:T(8,128)(2,1)S(1)} %get-tuple-element.9), channel_id=1, source_target_pairs={{0,8},{4,12},{8,16},{12,20},{16,24},{20,28},{1,9},{5,13},{9,17},{1... | collective-permute-start | bytes 983048 | tf_op jit(solution)/shard_map/ppermute | solution.py:20
  35.6 41.8 %copy-start.11 = (bf16[3,3,1,128,128]{4,3,2,1,0:T(8,128)(2,1)}, bf16[3,3,1,128,128]{4,3,2,1,0:T(8,128)(2,1)S(1)}, u32[]{:S(2)}) copy-start(bf16[3,3,1,128,128]{4,3,2,1,0:T(8,128)(2,1)S(1)} %get-tuple-element.19) | copy-start | bytes 884740
  35.6 41.8 %copy-start.12 = (bf16[3,3,1,128,128]{4,3,2,1,0:T(8,128)(2,1)}, bf16[3,3,1,128,128]{4,3,2,1,0:T(8,128)(2,1)S(1)}, u32[]{:S(2)}) copy-start(bf16[3,3,1,128,128]{4,3,2,1,0:T(8,128)(2,1)S(1)} %get-tuple-element.20) | copy-start | bytes 884740
  35.6 41.8 %copy-start.13 = (bf16[3,3,1,128,128]{4,3,2,1,0:T(8,128)(2,1)}, bf16[3,3,1,128,128]{4,3,2,1,0:T(8,128)(2,1)S(1)}, u32[]{:S(2)}) copy-start(bf16[3,3,1,128,128]{4,3,2,1,0:T(8,128)(2,1)S(1)} %get-tuple-element.21) | copy-start | bytes 884740
  44.4 12.9 %collective-permute-start.5 = (bf16[2,20,20,1,128]{4,3,2,1,0:T(2,128)(2,1)S(1)}, bf16[2,20,20,1,128]{4,3,2,1,0:T(2,128)(2,1)S(1)}, u32[]{:S(2)}, u32[]{:S(2)}) collective-permute-start(bf16[2,20,20,1,128]{4,3,2,1,0:T(2,128)(2,1)S(1)} %get-tuple-element.8), channel_id=1, source_target_pairs={{4,0},{8,4},{12,8},{16,12},{20,16},{24,20},{28,24},{5,1},{9,5},{13... | collective-permute-start | bytes 614408 | tf_op jit(solution)/shard_map/ppermute | solution.py:20
  46.2 20.0 %collective-permute-start.4 = (bf16[2,20,20,1,128]{4,3,2,1,0:T(2,128)(2,1)S(1)}, bf16[2,20,20,1,128]{4,3,2,1,0:T(2,128)(2,1)S(1)}, u32[]{:S(2)}, u32[]{:S(2)}) collective-permute-start(bf16[2,20,20,1,128]{4,3,2,1,0:T(2,128)(2,1)S(1)} %get-tuple-element.7), channel_id=1, source_target_pairs={{0,4},{4,8},{8,12},{12,16},{16,20},{20,24},{24,28},{1,5},{5,9},{9,... | collective-permute-start | bytes 614408 | tf_op jit(solution)/shard_map/ppermute | solution.py:20
  72.5 3.0 %copy-start = (bf16[2,20,20,18,128]{4,3,2,1,0:T(8,128)(2,1)}, bf16[2,20,20,18,128]{4,3,2,1,0:T(8,128)(2,1)S(1)}, u32[]{:S(2)}) copy-start(bf16[2,20,20,18,128]{4,3,2,1,0:T(8,128)(2,1)S(1)} %pad_maximum_fusion) | copy-start | bytes 11059204
  76.6 0.8 copy-start.18
  105.7 4.5 %copy-start.1 = (f32[18,18,1,24,128]{4,3,1,0,2:T(8,128)S(1)}, f32[18,18,1,24,128]{4,3,1,0,2:T(8,128)}, u32[]{:S(2)}) copy-start(f32[18,18,1,24,128]{4,3,1,0,2:T(8,128)} %reshape.72) | copy-start | bytes 11943940
  113.2 3.9 %copy-start.9 = (f32[18,18,8,3,128]{4,2,3,1,0:T(8,128)S(1)}, f32[18,18,8,3,128]{4,2,3,1,0:T(8,128)}, u32[]{:S(2)}) copy-start(f32[18,18,8,3,128]{4,2,3,1,0:T(8,128)} %get-tuple-element.26) | copy-start | bytes 11943940
  138.7 3.2 %copy-start.5 = (bf16[20,20,20,128]{3,2,1,0:T(8,128)(2,1)S(1)}, bf16[20,20,20,128]{3,2,1,0:T(8,128)(2,1)}, u32[]{:S(2)}) copy-start(bf16[20,20,20,128]{3,2,1,0:T(8,128)(2,1)} %get-tuple-element.5) | copy-start | bytes 6144004
  138.7 4.3 %copy-start.3 = (f32[18,18,18,128]{3,2,1,0:T(8,128)S(1)}, f32[18,18,18,128]{3,2,1,0:T(8,128)}, u32[]{:S(2)}) copy-start(f32[18,18,18,128]{3,2,1,0:T(8,128)} %add_divide_fusion) | copy-start | bytes 8957956
  139.1 1.3 copy-start.6
  140.3 3.8 %copy-start.2 = (f32[18,18,18,128]{3,2,1,0:T(8,128)S(1)}, f32[18,18,18,128]{3,2,1,0:T(8,128)}, u32[]{:S(2)}) copy-start(f32[18,18,18,128]{3,2,1,0:T(8,128)} %slice_bitcast_fusion.1) | copy-start | bytes 8957956
  180.7 1.9 copy-start.7
  180.7 2.2 copy-start.10
  180.7 2.2 copy-start.17
  182.0 100.2 %all-reduce.7.cloned.1.call-start = ((), (), s32[]{:S(2)}) async-start(), calls=%async_computation.2 | async-start | bytes 442368 | tf_op jit(solution)/shard_map/psum | solution.py:180
  196.8 1.6 copy-start.4
  197.0 11.1 %copy-start.8 = (bf16[1,16,8,8,512]{4,3,2,1,0:T(8,128)(2,1)S(1)}, bf16[1,16,8,8,512]{4,3,2,1,0:T(8,128)(2,1)}, u32[]{:S(2)}) copy-start(bf16[1,16,8,8,512]{4,3,2,1,0:T(8,128)(2,1)} %param.4) | copy-start | bytes 3145732
  197.0 11.1 %copy-start.15 = (f32[16]{0:T(128)S(1)}, f32[16]{0:T(128)}, u32[]{:S(2)}) copy-start(f32[16]{0:T(128)} %convert_bitcast_fusion.1) | copy-start | bytes 196
Sparse Core Ops, SparseCore 0:
  182.2 25.7 reduce-scatter.1
  211.4 70.8 all-reduce.6
